TPU v7x, 128 devices: a whole 4x4x4 slice. The times are simulated.
128 devices in a mesh: ctx: 4 (over x_hi, core), exp: 32 (over z, y, x_lo).
Axes of the slice: x: 4 (x_hi: 2, x_lo: 2; x = x_hi * 2 + x_lo), y: 4, z: 4, core: 2. Of those that a mesh axis runs over, the one named last changes fastest.
Arguments:
- queries: bfloat16 [4096, 8192], P('ctx', 'exp'), may hold values from -32 to 32
- keys: bfloat16 [4096, 8192], P('ctx', 'exp'), may hold values from -4 to 4
- values: bfloat16 [4096, 8192], P('ctx', 'exp'), may hold values from -6 to 6
- out_proj: bfloat16 [8192, 3584], P('exp'), may hold values from -0.5 to 0.5
- residual: bfloat16 [4096, 3584], P(('ctx', 'exp')), may hold values from -6 to 6
- norm_gain: float32 [3584], replicated, may hold values from 0.25 to 1.75
- routes: int32 [4096, 8], P(('ctx', 'exp')), may hold values from 0 to 31, all different within a row; in each aligned block of 32 rows (0 to 31, 32 to 63, ...) at most 10 rows name the same one
- combine: float32 [4096, 8], P(('ctx', 'exp')), may hold values from 0.1 to 0.5
- w_gate: bfloat16 [32, 3584, 1024], P('exp', None, 'ctx'), may hold values from -0.09375 to 0.09375
- w_up: bfloat16 [32, 3584, 1024], P('exp', None, 'ctx'), may hold values from -0.09375 to 0.09375
- w_down: bfloat16 [32, 1024, 3584], P('exp', 'ctx'), may hold values from -0.1875 to 0.1875
Outputs:
- layer_out: bfloat16 [4096, 3584], P(('ctx', 'exp'))
Inputs may be any that keep to these rules, and one draw needn't show every extreme that they name: `routes`: each row names 8 different experts. Within each aligned block of 32 rows no expert is named by more than 10 rows, and some block names some expert exactly 10 times.
All inputs are finite; a program needn't handle non-finite values.
Results may differ from a plain program's by a relative error of at most 0.023.
Values may be sent and summed in bfloat16 or wider, within the bound.
No kernel may reach another device: no remote copies, remote signals or barrier semaphores. Data moves between devices by JAX's collectives and lax.ppermute only.
A program may use at most 128 MiB of HBM per device.

v0:
```python
import math
import jax
import jax.numpy as jnp
from jax import lax
from jax.sharding import PartitionSpec as P

HD = 128
masked_score = -1e30
norm_eps = 1e-06


def from_behind(shard, axis, by):
    peers = lax.axis_size(axis)
    pairs = [(i, i + by) for i in range(peers) if 0 <= i + by < peers]
    return lax.ppermute(shard, axis, pairs)


def per_device(
    queries, keys, values, out_proj, residual, norm_gain, routes, combine, w_gate, w_up, w_down
):
    query_rows = queries.shape[0]
    head_count = queries.shape[1] // HD
    scaling = 1.0 / math.sqrt(HD)
    ctx_where = lax.axis_index("ctx")
    ctx_count = lax.axis_size("ctx")

    def attend(carried, query_heads, pair_block, visible):
        key_count = pair_block.shape[1]
        key_heads = pair_block[0].reshape(key_count, head_count, HD)
        value_heads = pair_block[1].reshape(key_count, head_count, HD)
        scores = (
            jnp.einsum("qhd,khd->hqk", query_heads, key_heads, preferred_element_type=jnp.float32)
            * scaling
        )
        scores = jnp.where(visible, scores, masked_score)
        peak_old, total_old, weighted_old = carried
        peak_new = jnp.maximum(peak_old, jnp.max(scores, axis=2))
        expo_block = jnp.exp(scores - peak_new[:, :, None])
        factor = jnp.exp(peak_old - peak_new)
        total_new = total_old * factor + jnp.sum(expo_block, axis=2)
        weighted_new = weighted_old * factor.T[:, :, None] + jnp.einsum(
            "hqk,khd->qhd",
            expo_block.astype(jnp.bfloat16),
            value_heads,
            preferred_element_type=jnp.float32,
        )
        return (peak_new, total_new, weighted_new)

    initial = (
        jnp.full((head_count, query_rows), masked_score, jnp.float32),
        jnp.zeros((head_count, query_rows), jnp.float32),
        jnp.zeros((query_rows, head_count, HD), jnp.float32),
    )
    query_heads = queries.reshape(query_rows, head_count, HD)
    row_ids = jnp.arange(query_rows)
    diag_mask = row_ids[:, None] >= row_ids[None, :]
    pair_block = jnp.stack([keys, values])
    carried = attend(initial, query_heads, pair_block, diag_mask)
    for step_index in range(1, ctx_count):
        pair_block = from_behind(pair_block, "ctx", 1)
        carried = attend(carried, query_heads, pair_block, ctx_where >= step_index)
    attended = (
        (carried[2] / carried[1].T[:, :, None])
        .astype(jnp.bfloat16)
        .reshape(query_rows, head_count * HD)
    )
    tok_count = residual.shape[0]
    term = jnp.dot(attended, out_proj, preferred_element_type=jnp.float32)
    mixed = lax.psum_scatter(
        lax.optimization_barrier(term.astype(jnp.bfloat16))
        .astype(jnp.float32)
        .astype(jnp.bfloat16),
        "exp",
        scatter_dimension=0,
        tiled=True,
    ).astype(jnp.float32)
    stream = residual.astype(jnp.float32) + mixed
    normed = (
        stream * lax.rsqrt(jnp.mean(stream * stream, axis=1, keepdims=True) + norm_eps) * norm_gain
    ).astype(jnp.bfloat16)
    width = normed.shape[1]
    per_token = routes.shape[1]
    experts = lax.axis_size("exp")
    capacity = min(tok_count, max(2, tok_count * per_token * 5 // (4 * experts)))
    pair_count = tok_count * per_token
    flat_routes = routes.reshape(pair_count)
    expert_hot = (flat_routes[:, None] == jnp.arange(experts)[None, :]).astype(jnp.int32)
    earlier = jnp.cumsum(expert_hot, axis=0) - expert_hot
    slot_index = jnp.sum(earlier * expert_hot, axis=1)
    position = flat_routes * capacity + slot_index
    position_hot = (position[:, None] == jnp.arange(experts * capacity)[None, :]).astype(
        jnp.float32
    )
    token_hot = (
        (jnp.arange(pair_count) // per_token)[:, None] == jnp.arange(tok_count)[None, :]
    ).astype(jnp.float32)
    pick_rows = jnp.einsum("pr,pt->rt", position_hot, token_hot).astype(jnp.bfloat16)
    outgoing = (
        jnp.dot(pick_rows, normed, preferred_element_type=jnp.float32)
        .astype(jnp.bfloat16)
        .reshape(experts, capacity, width)
    )
    received = lax.all_to_all(outgoing, "exp", split_axis=0, concat_axis=0, tiled=True)
    gate_local = w_gate[0]
    up_local = w_up[0]
    down_local = w_down[0]
    piece = lax.all_gather(received, "ctx", axis=0, tiled=True)
    gate = jnp.einsum("smd,df->smf", piece, gate_local, preferred_element_type=jnp.float32)
    upper = jnp.einsum("smd,df->smf", piece, up_local, preferred_element_type=jnp.float32)
    act_all = (jax.nn.silu(gate) * upper).astype(jnp.bfloat16)
    expert_out = lax.psum_scatter(
        jnp.einsum("smf,fd->smd", act_all, down_local, preferred_element_type=jnp.float32).astype(
            jnp.bfloat16
        ),
        "ctx",
        scatter_dimension=0,
        tiled=True,
    )
    returned = lax.all_to_all(expert_out, "exp", split_axis=0, concat_axis=0, tiled=True)
    weigh_rows = jnp.einsum(
        "pr,pt->tr", position_hot, token_hot * combine.reshape(pair_count)[:, None]
    )
    moe_sum = jnp.dot(
        weigh_rows,
        returned.reshape(experts * capacity, width).astype(jnp.float32),
        precision=lax.Precision.HIGHEST,
    )
    return (stream + moe_sum).astype(jnp.bfloat16)


def solution(mesh):
    in_specs = (
        P("ctx", "exp"),
        P("ctx", "exp"),
        P("ctx", "exp"),
        P("exp", None),
        P(("ctx", "exp"), None),
        P(),
        P(("ctx", "exp"), None),
        P(("ctx", "exp"), None),
        P("exp", None, "ctx"),
        P("exp", None, "ctx"),
        P("exp", "ctx", None),
    )
    out_specs = P(("ctx", "exp"), None)
    return jax.shard_map(
        per_device, mesh=mesh, in_specs=in_specs, out_specs=out_specs, check_vma=False
    )
```

profile of v0, /device:TPU:0, one launch (start us, length us, event | category | flops | bytes accessed | tf_op | source)
XLA Modules:
  0.0 577.8 jit_solution(9103200832604221513)
XLA Ops:
  9.3 2.5 collective-permute-start
  13.1 16.1 %collective-permute-start.1 = (bf16[2,1024,256]{1,2,0:T(8,128)(2,1)}, bf16[2,1024,256]{1,2,0:T(8,128)(2,1)}, u32[]{:S(2)}, u32[]{:S(2)}) collective-permute-start(bf16[2,1024,256]{1,2,0:T(8,128)(2,1)} %collective-permute-done), channel_id=1, source_target_pairs={{0,32},{32,64},{64,96},{1,33},{33,65},{65,97},{2,34},{34,66},{66,9... | collective-permute-start | bytes 3145736 | tf_op jit(solution)/shard_map/ppermute | solution.py:15
  29.5 6.3 %fusion.3 = (f32[2,1024]{1,0:T(2,128)S(1)}, f32[2,1024,1024]{1,2,0:T(8,128)}) fusion(pred[1024,1024]{0,1:T(8,128)(4,1)S(1)} %iota_compare_fusion, bf16[1024,256]{1,0:T(8,128)(2,1)} %param.12, bf16[1024,256]{1,0:T(8,128)(2,1)} %param.11), kind=kOutput, calls=%fused_computation.16 | convolution fusion | flops 543160320 | bytes 10493952 | tf_op jit(solution)/shard_map/qhd,khd->hqk/dot_general | solution.py:32
  37.1 9.3 %collective-permute-start.2 = (bf16[2,1024,256]{1,2,0:T(8,128)(2,1)}, bf16[2,1024,256]{1,2,0:T(8,128)(2,1)S(1)}, u32[]{:S(2)}, u32[]{:S(2)}) collective-permute-start(bf16[2,1024,256]{1,2,0:T(8,128)(2,1)} %collective-permute-done.1), channel_id=1, source_target_pairs={{0,32},{32,64},{64,96},{1,33},{33,65},{65,97},{2,34},{34,66},{66,9... | collective-permute-start | bytes 3145736 | tf_op jit(solution)/shard_map/ppermute | solution.py:15
  54.3 4.5 fusion.4
  58.8 4.0 fusion.6
  62.9 4.9 fusion.66
  67.7 2.6 fusion.57
  70.4 2.6 fusion.60
  75.5 5.1 convolution_convert_fusion.1
  81.8 201.2 %reduce-scatter.3.cloned.1.call-done = bf16[32,3584]{1,0:T(8,128)(2,1)} async-done(((bf16[1024,3584]{1,0:T(8,128)(2,1)}), bf16[32,3584]{1,0:T(8,128)(2,1)}) %reduce-scatter.3.cloned.1.call-update) | async-done | bytes 229392 | tf_op jit(solution)/shard_map/reduce_scatter | solution.py:69
  284.2 3.4 convolution_convert_fusion.2
  287.6 4.4 reshape.96
  292.0 33.5 %all_to_all.10 = bf16[32,10,3584]{2,1,0:T(8,128)(2,1)S(1)} all-to-all(bf16[32,10,3584]{2,1,0:T(8,128)(2,1)} %reshape.96), channel_id=1, replica_groups=mesh['ctx'=4,'exp'=32] {'exp'}, dimensions={0} | all-to-all | bytes 4587520 | tf_op jit(solution)/shard_map/all_to_all | solution.py:103
  325.5 2.7 copy.66
  328.2 64.2 %all-gather.2.cloned.1.call-done = bf16[128,10,3584]{2,0,1:T(8,128)(2,1)} async-done(((bf16[32,10,3584]{2,0,1:T(8,128)(2,1)}), bf16[128,10,3584]{2,0,1:T(8,128)(2,1)}) %all-gather.2.cloned.1.call-update) | async-done | bytes 9175056 | tf_op jit(solution)/shard_map/all_gather | solution.py:107
  392.4 7.7 %fusion.28 = f32[128,10,256]{2,0,1:T(8,128)} fusion(bf16[128,10,3584]{2,0,1:T(8,128)(2,1)} %all-gather.2.cloned.1.call-done, bf16[1,3584,256]{2,1,0:T(8,128)(2,1)} %param.19), kind=kOutput, calls=%fused_computation.40 | convolution fusion | flops 2348810240 | bytes 12320768 | tf_op jit(solution)/shard_map/smd,df->smf/dot_general | solution.py:108
  400.2 18.5 %convolution_convert_fusion = bf16[128,10,3584]{2,0,1:T(8,128)(2,1)} fusion(bf16[1,256,3584]{2,1,0:T(8,128)(2,1)S(1)} %copy-done, bf16[128,10,3584]{2,0,1:T(8,128)(2,1)} %all-gather.2.cloned.1.call-done, bf16[1,3584,256]{2,1,0:T(8,128)(2,1)} %param.20, f32[128,10,256]{2,0,1:T(8,128)} %fusion.28), kind=kOutput, calls=%fused_computation.14 | convolution fusion | flops 4704174080 | bytes 23330816 | tf_op jit(solution)/shard_map/smf,fd->smd/dot_general | solution.py:112
  418.7 82.6 %reduce-scatter.5.cloned.1.call-done = bf16[32,10,3584]{2,0,1:T(8,128)(2,1)} async-done(((bf16[128,10,3584]{2,0,1:T(8,128)(2,1)}), bf16[32,10,3584]{2,0,1:T(8,128)(2,1)}) %reduce-scatter.5.cloned.1.call-update) | async-done | bytes 2293776 | tf_op jit(solution)/shard_map/reduce_scatter | solution.py:111
  501.3 4.9 copy.67
  506.1 7.4 %all-to-all-start.1 = ((bf16[32,10,3584]{2,1,0:T(8,128)(2,1)}), bf16[32,10,3584]{2,1,0:T(8,128)(2,1)}, u32[]{:S(2)}, u32[]{:S(2)}) async-start(bf16[32,10,3584]{2,1,0:T(8,128)(2,1)} %copy.67), calls=%async_computation.3 | async-start | bytes 7340032 | tf_op jit(solution)/shard_map/all_to_all | solution.py:119
  514.0 49.2 %all-to-all-done.1 = bf16[32,10,3584]{2,1,0:T(8,128)(2,1)} async-done(((bf16[32,10,3584]{2,1,0:T(8,128)(2,1)}), bf16[32,10,3584]{2,1,0:T(8,128)(2,1)}, u32[]{:S(2)}, u32[]{:S(2)}) %all-to-all-start.1) | async-done | bytes 2293792 | tf_op jit(solution)/shard_map/all_to_all | solution.py:119
  563.2 4.5 reshape.97
  567.7 3.6 fusion.12
  (54 shorter events, 19.0 us)
Async XLA Ops:
  6.5 393.6 %copy-start = (bf16[1,256,3584]{2,1,0:T(8,128)(2,1)S(1)}, bf16[1,256,3584]{2,1,0:T(8,128)(2,1)}, u32[]{:S(2)}) copy-start(bf16[1,256,3584]{2,1,0:T(8,128)(2,1)} %param.21) | copy-start | bytes 5505028
  6.5 276.5 %reduce-scatter.3.cloned.1.call-start = ((), (), s32[]{:S(2)}) async-start(), calls=%async_computation.4 | async-start | bytes 7569408 | tf_op jit(solution)/shard_map/reduce_scatter | solution.py:69
  9.2 37.1 %copy-start.1 = (bf16[1024,256]{1,0:T(8,128)(2,1)S(1)}, bf16[1024,256]{1,0:T(8,128)(2,1)}, u32[]{:S(2)}) copy-start(bf16[1024,256]{1,0:T(8,128)(2,1)} %param.11) | copy-start | bytes 1572868
  9.3 3.8 collective-permute-start
  13.1 23.9 %collective-permute-start.1 = (bf16[2,1024,256]{1,2,0:T(8,128)(2,1)}, bf16[2,1024,256]{1,2,0:T(8,128)(2,1)}, u32[]{:S(2)}, u32[]{:S(2)}) collective-permute-start(bf16[2,1024,256]{1,2,0:T(8,128)(2,1)} %collective-permute-done), channel_id=1, source_target_pairs={{0,32},{32,64},{64,96},{1,33},{33,65},{65,97},{2,34},{34,66},{66,9... | collective-permute-start | bytes 3145736 | tf_op jit(solution)/shard_map/ppermute | solution.py:15
  37.1 13.4 %collective-permute-start.2 = (bf16[2,1024,256]{1,2,0:T(8,128)(2,1)}, bf16[2,1024,256]{1,2,0:T(8,128)(2,1)S(1)}, u32[]{:S(2)}, u32[]{:S(2)}) collective-permute-start(bf16[2,1024,256]{1,2,0:T(8,128)(2,1)} %collective-permute-done.1), channel_id=1, source_target_pairs={{0,32},{32,64},{64,96},{1,33},{33,65},{65,97},{2,34},{34,66},{66,9... | collective-permute-start | bytes 3145736 | tf_op jit(solution)/shard_map/ppermute | solution.py:15
  73.0 2.4 copy-start.4
  75.4 5.2 copy-start.6
  75.4 207.6 %copy-start.2 = (bf16[32,3584]{1,0:T(8,128)(2,1)S(1)}, bf16[32,3584]{1,0:T(8,128)(2,1)}, u32[]{:S(2)}) copy-start(bf16[32,3584]{1,0:T(8,128)(2,1)} %param.15) | copy-start | bytes 688132
  75.5 208.8 %copy-start.5 = (f32[3584]{0:T(1024)S(1)}, f32[3584]{0:T(1024)}, u32[]{:S(2)}) copy-start(f32[3584]{0:T(1024)} %param.16) | copy-start | bytes 43012
  80.6 311.9 %all-gather.2.cloned.1.call-start = ((), (), s32[]{:S(2)}) async-start(), calls=%async_computation.5 | async-start | bytes 11468800 | tf_op jit(solution)/shard_map/all_gather | solution.py:107
  328.2 173.1 %reduce-scatter.5.cloned.1.call-start = ((), (), s32[]{:S(2)}) async-start(), calls=%async_computation.6 | async-start | bytes 11468800 | tf_op jit(solution)/shard_map/reduce_scatter | solution.py:111
  418.6 94.9 %copy-start.7 = (f32[32,8]{0,1:T(8,128)S(1)}, f32[32,8]{0,1:T(8,128)}, u32[]{:S(2)}) copy-start(f32[32,8]{0,1:T(8,128)} %param.18) | copy-start | bytes 3076
  418.7 149.1 %copy-start.3 = (bf16[32,3584]{1,0:T(8,128)(2,1)S(1)}, bf16[32,3584]{1,0:T(8,128)(2,1)}, u32[]{:S(2)}) copy-start(bf16[32,3584]{1,0:T(8,128)(2,1)} %reduce-scatter.3.cloned.1.call-done) | copy-start | bytes 688132
  506.1 57.1 %all-to-all-start.1 = ((bf16[32,10,3584]{2,1,0:T(8,128)(2,1)}), bf16[32,10,3584]{2,1,0:T(8,128)(2,1)}, u32[]{:S(2)}, u32[]{:S(2)}) async-start(bf16[32,10,3584]{2,1,0:T(8,128)(2,1)} %copy.67), calls=%async_computation.3 | async-start | bytes 7340032 | tf_op jit(solution)/shard_map/all_to_all | solution.py:119
Sparse Core Ops, SparseCore 0:
  80.7 202.3 reduce-scatter.2
  328.3 64.0 all-gather.1
  418.8 82.4 reduce-scatter.4
where the time goes:
time: 579 us; the launch traced here: 578 us
  waiting for transfers between devices  399 us (69%)
  matrix products  61.7 us (11%)
  starting transfers between devices  35.3 us (6%)
  blocking collectives  33.5 us (6%)
  local copies, waits for them, and re-layouts  22.3 us (4%)
  between operations  13.4 us (2%)
  other arithmetic  13.1 us (2%)
    reduce_scatter x1, waiting for transfers between devices, per_device(): lax.psum_scatter(lax.optimization_barrier(term.astype(jnp.bfloat16)).asty...  201 us
    reduce_scatter x1, waiting for transfers between devices, per_device(): lax.psum_scatter(jnp.einsum('smf,fd->smd', act_all, down_local, preferred...  82.6 us
    all_gather x1, waiting for transfers between devices, per_device(): piece = lax.all_gather(received, 'ctx', axis=0, tiled=True)  64.2 us
    all_to_all x1, waiting for transfers between devices, per_device(): lax.all_to_all(expert_out, 'exp', split_axis=0, concat_axis=0, tiled=True)  49.2 us
    all_to_all x1, blocking collectives, per_device(): lax.all_to_all(outgoing, 'exp', split_axis=0, concat_axis=0, tiled=True)  33.5 us
    ppermute x3, starting transfers between devices, from_behind(): return lax.ppermute(shard, axis, pairs)  27.8 us
    dot_general x1, matrix products, per_device(): jnp.einsum('smf,fd->smd', act_all, down_local, preferred_element_type=jnp...  18.5 us
    dot_general x4, matrix products, attend(): jnp.einsum('hqk,khd->qhd', expo_block.astype(jnp.bfloat16), value_heads,...  12.5 us
  transfers between devices with their start and end apart: 7, of which 5 were waited for; matrix products, arithmetic and copies ran while one was open for 2% of the time, Pallas kernels for 0%

commit v1 on v0

--- a/solution.py
+++ b/solution.py
@@ -104,7 +104,9 @@
     gate_local = w_gate[0]
     up_local = w_up[0]
     down_local = w_down[0]
-    piece = lax.all_gather(received, "ctx", axis=0, tiled=True)
+    piece = jnp.concatenate(
+        lax.all_to_all(jnp.stack([received] * lax.axis_size("ctx")), "ctx", 0, 0), axis=0
+    )
     gate = jnp.einsum("smd,df->smf", piece, gate_local, preferred_element_type=jnp.float32)
     upper = jnp.einsum("smd,df->smf", piece, up_local, preferred_element_type=jnp.float32)
     act_all = (jax.nn.silu(gate) * upper).astype(jnp.bfloat16)

time: 579 us -> 628 us (1.085)
  blocking collectives: 33.5 us -> 140 us
  waiting for transfers between devices: 399 us -> 330 us
  local copies, waits for them, and re-layouts: 22.3 us -> 33.2 us
    all_to_all x0 -> x1, blocking collectives: none -> 107 us  [per_device(): lax.all_to_all(jnp.stack([received] * lax.axis_size('ctx')), 'ctx', 0, 0)]
    all_gather x1 -> x0, waiting for transfers between devices: 64.2 us -> none  [per_device(): piece = lax.all_gather(received, 'ctx', axis=0, tiled=True)]
    all_to_all x0 -> x1, local copies, waits for them, and re-layouts: none -> 8.15 us  [per_device(): lax.all_to_all(jnp.stack([received] * lax.axis_size('ctx')), 'ctx', 0, 0)]
  transfers between devices with their start and end apart: 7 -> 6, of which waited for: 5 -> 4; matrix products, arithmetic and copies ran while one was open for 2% -> 2% of each run, Pallas kernels for 0% -> 0%
where the time goes in v1:
time: 628 us
  waiting for transfers between devices  330 us (53%)
  blocking collectives  140 us (22%)
  matrix products  61.7 us (10%)
  starting transfers between devices  35.3 us (6%)
  local copies, waits for them, and re-layouts  33.2 us (5%)
  between operations  13.7 us (2%)
  other arithmetic  13.1 us (2%)
    reduce_scatter x1, waiting for transfers between devices, per_device(): lax.psum_scatter(lax.optimization_barrier(term.astype(jnp.bfloat16)).asty...  201 us
    all_to_all x1, blocking collectives, per_device(): lax.all_to_all(jnp.stack([received] * lax.axis_size('ctx')), 'ctx', 0, 0)  107 us
    reduce_scatter x1, waiting for transfers between devices, per_device(): lax.psum_scatter(jnp.einsum('smf,fd->smd', act_all, down_local, preferred...  78.5 us
    all_to_all x1, waiting for transfers between devices, per_device(): lax.all_to_all(expert_out, 'exp', split_axis=0, concat_axis=0, tiled=True)  49.3 us
    all_to_all x1, blocking collectives, per_device(): lax.all_to_all(outgoing, 'exp', split_axis=0, concat_axis=0, tiled=True)  33.5 us
    ppermute x3, starting transfers between devices, from_behind(): return lax.ppermute(shard, axis, pairs)  27.8 us
    dot_general x1, matrix products, per_device(): jnp.einsum('smf,fd->smd', act_all, down_local, preferred_element_type=jnp...  18.5 us
  transfers between devices with their start and end apart: 6, of which 4 were waited for; matrix products, arithmetic and copies ran while one was open for 2% of the time, Pallas kernels for 0%

profile of v1, /device:TPU:0, one launch (start us, length us, event | category | flops | bytes accessed | tf_op | source)
XLA Modules:
  0.0 627.5 jit_solution(12059499278909528783)
XLA Ops:
  13.1 16.1 %collective-permute-start.1 = (bf16[2,1024,256]{1,2,0:T(8,128)(2,1)}, bf16[2,1024,256]{1,2,0:T(8,128)(2,1)}, u32[]{:S(2)}, u32[]{:S(2)}) collective-permute-start(bf16[2,1024,256]{1,2,0:T(8,128)(2,1)} %collective-permute-done), channel_id=1, source_target_pairs={{0,32},{32,64},{64,96},{1,33},{33,65},{65,97},{2,34},{34,66},{66,9... | collective-permute-start | bytes 3145736 | tf_op jit(solution)/shard_map/ppermute | solution.py:15
  29.5 6.3 fusion.3
  37.1 9.3 %collective-permute-start.2 = (bf16[2,1024,256]{1,2,0:T(8,128)(2,1)}, bf16[2,1024,256]{1,2,0:T(8,128)(2,1)S(1)}, u32[]{:S(2)}, u32[]{:S(2)}) collective-permute-start(bf16[2,1024,256]{1,2,0:T(8,128)(2,1)} %collective-permute-done.1), channel_id=1, source_target_pairs={{0,32},{32,64},{64,96},{1,33},{33,65},{65,97},{2,34},{34,66},{66,9... | collective-permute-start | bytes 3145736 | tf_op jit(solution)/shard_map/ppermute | solution.py:15
  54.3 4.5 fusion.4
  58.8 4.0 fusion.6
  62.9 4.9 fusion.66
  70.4 2.6 fusion.60
  75.5 5.1 convolution_convert_fusion.1
  81.8 201.2 %reduce-scatter.3.cloned.1.call-done = bf16[32,3584]{1,0:T(8,128)(2,1)} async-done(((bf16[1024,3584]{1,0:T(8,128)(2,1)}), bf16[32,3584]{1,0:T(8,128)(2,1)}) %reduce-scatter.3.cloned.1.call-update) | async-done | bytes 229392 | tf_op jit(solution)/shard_map/reduce_scatter | solution.py:69
  284.2 3.4 convolution_convert_fusion.2
  287.6 4.4 reshape.101
  292.0 33.5 %all_to_all.15 = bf16[32,10,3584]{2,1,0:T(8,128)(2,1)S(1)} all-to-all(bf16[32,10,3584]{2,1,0:T(8,128)(2,1)} %reshape.101), channel_id=1, replica_groups=mesh['ctx'=4,'exp'=32] {'exp'}, dimensions={0} | all-to-all | bytes 4587520 | tf_op jit(solution)/shard_map/all_to_all | solution.py:103
  325.5 2.6 copy.66
  328.1 2.7 stack.19
  330.9 106.9 %all_to_all.16 = bf16[4,32,10,3584]{3,1,2,0:T(8,128)(2,1)} all-to-all(bf16[4,32,10,3584]{3,1,2,0:T(8,128)(2,1)S(1)} %stack.19), channel_id=1, replica_groups=mesh['ctx'=4,'exp'=32] {'ctx'}, dimensions={0} | all-to-all | bytes 18350080 | tf_op jit(solution)/shard_map/all_to_all | solution.py:108
  437.7 8.2 %copy.67 = bf16[4,32,10,3584]{3,1,0,2:T(8,128)(2,1)} copy(bf16[4,32,10,3584]{3,1,2,0:T(8,128)(2,1)} %all_to_all.16) | data formatting | bytes 18350080 | tf_op jit(solution)/shard_map/all_to_all | solution.py:108
  445.9 7.7 %fusion.28 = f32[128,10,256]{2,0,1:T(8,128)} fusion(bf16[128,10,3584]{2,0,1:T(8,128)(2,1)} %bitcast.237, bf16[1,3584,256]{2,1,0:T(8,128)(2,1)} %param.19), kind=kOutput, calls=%fused_computation.40 | convolution fusion | flops 2348810240 | bytes 12320768 | tf_op jit(solution)/shard_map/smd,df->smf/dot_general | solution.py:110
  453.6 18.5 %convolution_convert_fusion = bf16[128,10,3584]{2,0,1:T(8,128)(2,1)} fusion(bf16[1,256,3584]{2,1,0:T(8,128)(2,1)S(1)} %copy-done, bf16[128,10,3584]{2,0,1:T(8,128)(2,1)} %bitcast.238, bf16[1,3584,256]{2,1,0:T(8,128)(2,1)} %param.20, f32[128,10,256]{2,0,1:T(8,128)} %fusion.28), kind=kOutput, calls=%fused_computation.14 | convolution fusion | flops 4704174080 | bytes 23330816 | tf_op jit(solution)/shard_map/smf,fd->smd/dot_general | solution.py:114
  472.1 78.5 %reduce-scatter.5.cloned.1.call-done = bf16[32,10,3584]{2,0,1:T(8,128)(2,1)} async-done(((bf16[128,10,3584]{2,0,1:T(8,128)(2,1)}), bf16[32,10,3584]{2,0,1:T(8,128)(2,1)}) %reduce-scatter.5.cloned.1.call-update) | async-done | bytes 2293776 | tf_op jit(solution)/shard_map/reduce_scatter | solution.py:113
  550.6 4.9 copy.68
  555.5 7.4 %all-to-all-start.2 = ((bf16[32,10,3584]{2,1,0:T(8,128)(2,1)}), bf16[32,10,3584]{2,1,0:T(8,128)(2,1)}, u32[]{:S(2)}, u32[]{:S(2)}) async-start(bf16[32,10,3584]{2,1,0:T(8,128)(2,1)} %copy.68), calls=%async_computation.4 | async-start | bytes 7340032 | tf_op jit(solution)/shard_map/all_to_all | solution.py:121
  563.4 49.3 %all-to-all-done.2 = bf16[32,10,3584]{2,1,0:T(8,128)(2,1)} async-done(((bf16[32,10,3584]{2,1,0:T(8,128)(2,1)}), bf16[32,10,3584]{2,1,0:T(8,128)(2,1)}, u32[]{:S(2)}, u32[]{:S(2)}) %all-to-all-start.2) | async-done | bytes 2293792 | tf_op jit(solution)/shard_map/all_to_all | solution.py:121
  612.6 4.5 reshape.103
  617.1 3.6 fusion.12
  (54 shorter events, 24.1 us)
Async XLA Ops:
  6.5 447.1 %copy-start = (bf16[1,256,3584]{2,1,0:T(8,128)(2,1)S(1)}, bf16[1,256,3584]{2,1,0:T(8,128)(2,1)}, u32[]{:S(2)}) copy-start(bf16[1,256,3584]{2,1,0:T(8,128)(2,1)} %param.21) | copy-start | bytes 5505028
  6.5 276.5 %reduce-scatter.3.cloned.1.call-start = ((), (), s32[]{:S(2)}) async-start(), calls=%async_computation.5 | async-start | bytes 7569408 | tf_op jit(solution)/shard_map/reduce_scatter | solution.py:69
  9.2 37.1 %copy-start.1 = (bf16[1024,256]{1,0:T(8,128)(2,1)S(1)}, bf16[1024,256]{1,0:T(8,128)(2,1)}, u32[]{:S(2)}) copy-start(bf16[1024,256]{1,0:T(8,128)(2,1)} %param.11) | copy-start | bytes 1572868
  9.3 3.8 collective-permute-start
  13.1 23.9 %collective-permute-start.1 = (bf16[2,1024,256]{1,2,0:T(8,128)(2,1)}, bf16[2,1024,256]{1,2,0:T(8,128)(2,1)}, u32[]{:S(2)}, u32[]{:S(2)}) collective-permute-start(bf16[2,1024,256]{1,2,0:T(8,128)(2,1)} %collective-permute-done), channel_id=1, source_target_pairs={{0,32},{32,64},{64,96},{1,33},{33,65},{65,97},{2,34},{34,66},{66,9... | collective-permute-start | bytes 3145736 | tf_op jit(solution)/shard_map/ppermute | solution.py:15
  37.1 13.4 %collective-permute-start.2 = (bf16[2,1024,256]{1,2,0:T(8,128)(2,1)}, bf16[2,1024,256]{1,2,0:T(8,128)(2,1)S(1)}, u32[]{:S(2)}, u32[]{:S(2)}) collective-permute-start(bf16[2,1024,256]{1,2,0:T(8,128)(2,1)} %collective-permute-done.1), channel_id=1, source_target_pairs={{0,32},{32,64},{64,96},{1,33},{33,65},{65,97},{2,34},{34,66},{66,9... | collective-permute-start | bytes 3145736 | tf_op jit(solution)/shard_map/ppermute | solution.py:15
  73.0 2.4 copy-start.4
  75.4 5.2 copy-start.6
  75.4 207.6 %copy-start.2 = (bf16[32,3584]{1,0:T(8,128)(2,1)S(1)}, bf16[32,3584]{1,0:T(8,128)(2,1)}, u32[]{:S(2)}) copy-start(bf16[32,3584]{1,0:T(8,128)(2,1)} %param.15) | copy-start | bytes 688132
  75.5 208.8 %copy-start.5 = (f32[3584]{0:T(1024)S(1)}, f32[3584]{0:T(1024)}, u32[]{:S(2)}) copy-start(f32[3584]{0:T(1024)} %param.16) | copy-start | bytes 43012
  80.6 470.0 %reduce-scatter.5.cloned.1.call-start = ((), (), s32[]{:S(2)}) async-start(), calls=%async_computation.6 | async-start | bytes 11468800 | tf_op jit(solution)/shard_map/reduce_scatter | solution.py:113
  472.1 90.7 %copy-start.7 = (f32[32,8]{0,1:T(8,128)S(1)}, f32[32,8]{0,1:T(8,128)}, u32[]{:S(2)}) copy-start(f32[32,8]{0,1:T(8,128)} %param.18) | copy-start | bytes 3076
  472.1 145.0 %copy-start.3 = (bf16[32,3584]{1,0:T(8,128)(2,1)S(1)}, bf16[32,3584]{1,0:T(8,128)(2,1)}, u32[]{:S(2)}) copy-start(bf16[32,3584]{1,0:T(8,128)(2,1)} %reduce-scatter.3.cloned.1.call-done) | copy-start | bytes 688132
  555.5 57.2 %all-to-all-start.2 = ((bf16[32,10,3584]{2,1,0:T(8,128)(2,1)}), bf16[32,10,3584]{2,1,0:T(8,128)(2,1)}, u32[]{:S(2)}, u32[]{:S(2)}) async-start(bf16[32,10,3584]{2,1,0:T(8,128)(2,1)} %copy.68), calls=%async_computation.4 | async-start | bytes 7340032 | tf_op jit(solution)/shard_map/all_to_all | solution.py:121
Sparse Core Ops, SparseCore 0:
  80.7 202.3 reduce-scatter.2
  472.2 78.3 reduce-scatter.4
